TPU v7x, 256 devices: a whole 4x4x8 slice. The times are simulated.
256 devices in a mesh: section: 2 (over core), patch: 4 (over y), req: 32 (over z, x).
Axes of the slice: x: 4, y: 4, z: 8, core: 2. Of those that a mesh axis runs over, the one named last changes fastest.
Arguments:
- hidden: bfloat16 [64, 1024, 1536], P('req', 'patch'), may hold values from -6 to 6
- w_qkv: bfloat16 [2, 1536, 2304], P('section', ('patch', 'req')), may hold values from -0.15625 to 0.15625
- w_out: bfloat16 [2, 768, 1536], P('section', ('patch', 'req')), may hold values from -0.21875 to 0.21875
- modulation: float32 [2, 64, 3, 1536], P('section', 'req'), may hold values from -3 to 3
- text_kv: bfloat16 [2, 64, 160, 1536], P('section', 'req'), may hold values from -1000 to 1000
- text_lengths: int32 [64], P('req'), may hold values from 77 to 154, as said below
- stale_kv: bfloat16 [2, 64, 1024, 1536], P('section', 'req', 'patch'), may hold values from -48 to 48
- held_hidden: bfloat16 [2, 64, 96, 1536], P('section', 'req', 'patch'), may hold values from -6 to 6
- recompute_rows: int32 [2, 64, 96], P('section', 'req', 'patch'), may hold values from 0 to 255, as said below
- coefficients: float32 [64, 2], P('req'), may hold values from 0.5 to 1.5
Outputs:
- latents: float32 [64, 1024, 1536], P('req', 'patch', 'section')
- cache: bfloat16 [2, 64, 1024, 1536], P('section', 'req', 'patch')
Inputs may be any that keep to these rules, and one draw needn't show every extreme that they name: `text_lengths`: some request has exactly 154 text tokens and some exactly 77. `recompute_rows`: the row numbers listed for one layer, request and patch are distinct.
All inputs are finite; a program needn't handle non-finite values.
Results may differ from a plain program's by a relative error of at most 0.025.
Values may be sent and summed in bfloat16 or wider, within the bound.
No kernel may reach another device: no remote copies, remote signals or barrier semaphores. Data moves between devices by JAX's collectives and lax.ppermute only.
A program may use at most 128 MiB of HBM per device.

v0:
```python
import jax
import jax.numpy as jnp
from jax import lax
from jax.sharding import PartitionSpec as P

HEADS = 12


norm_eps = 1e-06
score_scale = 0.125


def shifted(block, axis, distance):
    devices = range(lax.axis_size(axis))
    route = [(i - distance, i) for i in devices if i - distance in devices]
    return lax.ppermute(block, axis, route)


def modulate(row_block, shift_row, scale_row):
    values = row_block.astype(jnp.float32)
    centre = values - jnp.mean(values, axis=-1, keepdims=True)
    spread = jnp.mean(centre * centre, axis=-1, keepdims=True)
    return (centre * lax.rsqrt(spread + norm_eps) * (1.0 + scale_row) + shift_row).astype(
        jnp.bfloat16
    )


def attend(queries, key_rows, value_rows, usable):
    row_count = queries.shape[0]
    feature_count = queries.shape[1]
    query_heads = queries.reshape(row_count, HEADS, feature_count // HEADS)
    key_heads = key_rows.reshape(key_rows.shape[0], HEADS, feature_count // HEADS)
    value_heads = value_rows.reshape(value_rows.shape[0], HEADS, feature_count // HEADS)
    scores = (
        jnp.einsum("qhd,khd->hqk", query_heads, key_heads, preferred_element_type=jnp.float32)
        * score_scale
    )
    scores = jnp.where(usable[None, None, :], scores, -1e30)
    row_max = jnp.max(scores, axis=-1, keepdims=True)
    exp_scores = jnp.exp(scores - row_max)
    soft_weights = (exp_scores / jnp.sum(exp_scores, axis=-1, keepdims=True)).astype(jnp.bfloat16)
    attended = jnp.einsum(
        "hqk,khd->qhd", soft_weights, value_heads, preferred_element_type=jnp.float32
    )
    return attended.reshape(row_count, feature_count).astype(jnp.bfloat16)


def body(
    hidden,
    w_qkv,
    w_out,
    modulation,
    text_kv,
    text_lengths,
    stale_kv,
    held_hidden,
    recompute_rows,
    coefficients,
):
    full_qkv, full_out = (
        lax.all_gather(w_qkv[0], ("patch", "req"), axis=0, tiled=True),
        lax.all_gather(w_out[0], ("patch", "req"), axis=0, tiled=True),
    )
    section_index = lax.axis_index("section")
    patch_index = lax.axis_index("patch")
    request_count = hidden.shape[0]
    patch_rows = hidden.shape[1]
    model_width = hidden.shape[2]
    head_width = full_out.shape[0]
    text_slots = text_kv.shape[2]

    def process(layer_input, slot_index):
        mod_rows = lax.dynamic_index_in_dim(modulation[0], slot_index, 0, keepdims=False)
        text_rows = lax.dynamic_index_in_dim(text_kv[0], slot_index, 0, keepdims=False)
        text_count = lax.dynamic_index_in_dim(text_lengths, slot_index, 0, keepdims=False)
        stale_block = lax.dynamic_index_in_dim(stale_kv[0], slot_index, 0, keepdims=False)
        held_rows = lax.dynamic_index_in_dim(held_hidden[0], slot_index, 0, keepdims=False)
        redo_index = lax.dynamic_index_in_dim(recompute_rows[0], slot_index, 0, keepdims=False)
        held_norm = modulate(held_rows, mod_rows[0], mod_rows[1])
        redone = jnp.dot(
            held_norm, full_qkv[:, head_width:], preferred_element_type=jnp.float32
        ).astype(jnp.bfloat16)
        patched = stale_block.at[redo_index].set(redone)
        image_rows = lax.all_gather(patched, "patch", axis=0, tiled=True)
        normed = modulate(layer_input, mod_rows[0], mod_rows[1])
        projected = jnp.dot(normed, full_qkv, preferred_element_type=jnp.float32).astype(
            jnp.bfloat16
        )
        fresh_rows = projected[:, head_width:]
        image_rows = lax.dynamic_update_slice_in_dim(
            image_rows, fresh_rows, patch_index * patch_rows, 0
        )
        context = jnp.concatenate([text_rows, image_rows], axis=0)
        usable = jnp.concatenate(
            [jnp.arange(text_slots) < text_count, jnp.ones((image_rows.shape[0],), jnp.bool_)]
        )
        attended = attend(
            projected[:, :head_width], context[:, :head_width], context[:, head_width:], usable
        )
        update = jnp.dot(attended, full_out, preferred_element_type=jnp.float32)
        layer_out = (layer_input.astype(jnp.float32) + mod_rows[2] * update).astype(jnp.bfloat16)
        return (layer_out, fresh_rows)

    first_pass = [process(hidden[slot_number], slot_number) for slot_number in range(request_count)]
    first_out = jnp.stack([entry[0] for entry in first_pass])
    first_fresh = jnp.stack([entry[1] for entry in first_pass])
    received = shifted(first_out, "section", 1)
    second_pass = [
        process(received[slot_number], slot_number) for slot_number in range(request_count)
    ]
    second_out = jnp.stack([entry[0] for entry in second_pass])
    second_fresh = jnp.stack([entry[1] for entry in second_pass])
    fresh_all = jnp.where(section_index == 0, first_fresh, second_fresh)
    half_width = model_width // 2
    returned = shifted(second_out[:, :, :half_width], "section", -1)
    own_half = jnp.where(section_index == 0, returned, second_out[:, :, half_width:])
    source_half = lax.dynamic_slice_in_dim(hidden, section_index * half_width, half_width, 2)
    latents = coefficients[:, 0][:, None, None] * source_half.astype(jnp.float32) + coefficients[
        :, 1
    ][:, None, None] * own_half.astype(jnp.float32)
    return (latents, fresh_all[None])


def solution(mesh):
    return jax.shard_map(
        body,
        mesh=mesh,
        in_specs=(
            P("req", "patch", None),
            P("section", ("patch", "req"), None),
            P("section", ("patch", "req"), None),
            P("section", "req", None, None),
            P("section", "req", None, None),
            P("req"),
            P("section", "req", "patch", None),
            P("section", "req", "patch", None),
            P("section", "req", "patch"),
            P("req", None),
        ),
        out_specs=(P("req", "patch", "section"), P("section", "req", "patch", None)),
        check_vma=False,
    )
```

profile of v0, /device:TPU:1, one launch (start us, length us, event | category | flops | bytes accessed | tf_op | source)
XLA Modules:
  0.0 496.8 jit_solution(3415797970322674418)
XLA Ops:
  7.2 1.6 copy.50
  8.9 1.4 copy.54
  14.2 1.5 slice_bitcast_fusion
  15.7 140.7 %all-gather.11.cloned.1.call-done = bf16[1,1536,2304]{2,0,1:T(2,128)(2,1)} async-done(((bf16[1,12,2304]{2,0,1:T(2,128)(2,1)}), bf16[1,1536,2304]{2,0,1:T(2,128)(2,1)}) %all-gather.11.cloned.1.call-update) | async-done | bytes 7077904 | tf_op jit(solution)/shard_map/all_gather | solution.py:61
  156.4 9.0 %copy.67 = bf16[1,1536,2304]{2,1,0:T(8,128)(2,1)} copy(bf16[1,1536,2304]{2,0,1:T(2,128)(2,1)} %all-gather.11.cloned.1.call-done) | data formatting | bytes 14155776
  165.4 3.1 fusion.52
  170.7 3.2 fusion.55
  173.9 1.7 scatter_fusion.1
  179.3 1.2 slice_bitcast_fusion.7
  180.5 91.4 %all-gather.13.cloned.1.call-done = bf16[1,768,1536]{2,0,1:T(2,128)(2,1)} async-done(((bf16[1,6,1536]{2,0,1:T(2,128)(2,1)}), bf16[1,768,1536]{2,0,1:T(2,128)(2,1)}) %all-gather.13.cloned.1.call-update) | async-done | bytes 2359312 | tf_op jit(solution)/shard_map/all_gather | solution.py:62
  271.9 3.0 copy.65
  275.0 5.2 %convolution_convert_fusion.3 = bf16[256,2304]{1,0:T(8,128)(2,1)S(1)} fusion(bf16[1536,2304]{1,0:T(8,128)(2,1)} %bitcast.210, f32[1536]{0:T(1024)S(1)} %get-tuple-element.16, f32[1536]{0:T(1024)S(1)} %get-tuple-element.17, f32[256]{0:T(256)S(1)} %add_rsqrt_fusion.3, f32[256]{0:T(256)S(1)} %broadcast_multiply_fusion.3, bf16[2,256,1536]{2,1,0:T(8,128)(2,1)S(1)} %copy-done.1), kind=kOutput, calls=%fused_computation.46 | convolution fusion | flops 1814888448 | bytes 9062400 | tf_op jit(solution)/shard_map/dot_general | solution.py:86
  282.0 1.9 copy.52
  283.9 5.7 %convolution_convert_fusion.2 = bf16[256,2304]{1,0:T(8,128)(2,1)S(1)} fusion(bf16[1536,2304]{1,0:T(8,128)(2,1)} %bitcast.211, f32[1536]{0:T(1024)S(1)} %get-tuple-element.18, f32[1536]{0:T(1024)S(1)} %get-tuple-element.19, f32[256]{0:T(256)S(1)} %add_rsqrt_fusion.2, f32[256]{0:T(256)S(1)} %broadcast_multiply_fusion.2, bf16[2,256,1536]{2,1,0:T(8,128)(2,1)} %param.10), kind=kOutput, calls=%fused_computation.45 | convolution fusion | flops 1814888448 | bytes 9058304 | tf_op jit(solution)/shard_map/dot_general | solution.py:86
  291.4 1.9 copy.56
  293.3 23.1 %all-gather.7.cloned.1.call-done = bf16[1024,1536]{1,0:T(8,128)(2,1)} async-done(((bf16[256,1536]{1,0:T(8,128)(2,1)}), bf16[1024,1536]{1,0:T(8,128)(2,1)}) %all-gather.7.cloned.1.call-update) | async-done | bytes 3145744 | tf_op jit(solution)/shard_map/all_gather | solution.py:84
  316.4 3.9 copy.73
  321.3 2.1 pad_maximum_fusion.3
  323.4 3.9 copy.53
  327.3 4.0 copy.51
  331.3 29.1 %all-gather.9.cloned.1.call-done = bf16[1024,1536]{1,0:T(8,128)(2,1)} async-done(((bf16[256,1536]{1,0:T(8,128)(2,1)}), bf16[1024,1536]{1,0:T(8,128)(2,1)}) %all-gather.9.cloned.1.call-update) | async-done | bytes 3145744 | tf_op jit(solution)/shard_map/all_gather | solution.py:84
  360.4 3.9 copy.72
  365.4 2.0 pad_maximum_fusion.1
  367.4 3.9 copy.57
  371.4 4.1 copy.55
  375.4 6.9 %fusion.178 = f32[12,256]{1,0:T(8,128)S(1)} fusion(pred[1184]{0:T(1024)(128)(4,1)S(1)} %concatenate.35, bf16[256,12,64]{0,2,1:T(8,128)(2,1)} %bitcast.232, bf16[1184,12,64]{0,2,1:T(8,128)(2,1)} %bitcast.216), kind=kOutput, calls=%fused_computation.243 | convolution fusion | flops 480117920 | bytes 2225312 | tf_op jit(solution)/shard_map/sub | solution.py:40
  382.3 9.5 %fusion.93 = bf16[12,64,256]{2,1,0:T(8,128)(2,1)} fusion(bf16[1184,12,64]{0,2,1:T(8,128)(2,1)} %bitcast.218, f32[12,256]{1,0:T(8,128)S(1)} %fusion.178, pred[1184]{0:T(1024)(128)(4,1)S(1)} %concatenate.35, bf16[256,12,64]{0,2,1:T(8,128)(2,1)} %bitcast.233, bf16[1184,12,64]{0,2,1:T(8,128)(2,1)} %bitcast.217), kind=kOutput, calls=%fused_computation.131 | convolution fusion | flops 949522560 | bytes 4437152 | tf_op jit(solution)/shard_map/hqk,khd->qhd/dot_general | solution.py:42
  391.8 7.1 %fusion.177 = f32[12,256]{1,0:T(8,128)S(1)} fusion(pred[1184]{0:T(1024)(128)(4,1)S(1)} %concatenate.37, bf16[256,12,64]{0,2,1:T(8,128)(2,1)} %bitcast.234, bf16[1184,12,64]{0,2,1:T(8,128)(2,1)} %bitcast.223), kind=kOutput, calls=%fused_computation.242 | convolution fusion | flops 480117920 | bytes 2225312 | tf_op jit(solution)/shard_map/sub | solution.py:40
  398.9 9.4 %fusion.92 = bf16[12,64,256]{2,1,0:T(8,128)(2,1)} fusion(bf16[1184,12,64]{0,2,1:T(8,128)(2,1)} %bitcast.227, f32[12,256]{1,0:T(8,128)S(1)} %fusion.177, pred[1184]{0:T(1024)(128)(4,1)S(1)} %concatenate.37, bf16[256,12,64]{0,2,1:T(8,128)(2,1)} %bitcast.235, bf16[1184,12,64]{0,2,1:T(8,128)(2,1)} %bitcast.224), kind=kOutput, calls=%fused_computation.130 | convolution fusion | flops 949522560 | bytes 4437152 | tf_op jit(solution)/shard_map/hqk,khd->qhd/dot_general | solution.py:42
  408.3 2.2 fusion.39
  410.5 2.3 fusion.38
  413.0 1.3 collective-permute-start
  414.3 4.0 collective-permute-done
  419.2 2.2 convolution_convert_fusion
  422.7 2.2 convolution_convert_fusion.1
  426.0 3.5 pad_maximum_fusion
  429.5 4.0 copy.63
  433.7 4.1 copy.61
  437.7 4.0 copy.60
  441.9 4.1 copy.58
  446.0 6.7 %fusion.180 = f32[12,256]{1,0:T(8,128)S(1)} fusion(pred[1184]{0:T(1024)(128)(4,1)S(1)} %copy-done.30, bf16[256,12,64]{0,2,1:T(8,128)(2,1)S(1)} %bitcast.238, bf16[1184,12,64]{0,2,1:T(8,128)(2,1)} %bitcast.221), kind=kOutput, calls=%fused_computation.245 | convolution fusion | flops 480117920 | bytes 2225312 | tf_op jit(solution)/shard_map/sub | solution.py:40
  452.7 8.7 %fusion.90 = bf16[12,64,256]{2,1,0:T(8,128)(2,1)S(1)} fusion(bf16[1184,12,64]{0,2,1:T(8,128)(2,1)} %bitcast.225, f32[12,256]{1,0:T(8,128)S(1)} %fusion.180, pred[1184]{0:T(1024)(128)(4,1)S(1)} %copy-done.30, bf16[256,12,64]{0,2,1:T(8,128)(2,1)} %bitcast.239, bf16[1184,12,64]{0,2,1:T(8,128)(2,1)} %bitcast.222), kind=kOutput, calls=%fused_computation.128 | convolution fusion | flops 949522560 | bytes 4437152 | tf_op jit(solution)/shard_map/hqk,khd->qhd/dot_general | solution.py:42
  461.4 7.0 %fusion.179 = f32[12,256]{1,0:T(8,128)S(1)} fusion(pred[1184]{0:T(1024)(128)(4,1)S(1)} %copy-done.28, bf16[256,12,64]{0,2,1:T(8,128)(2,1)S(1)} %bitcast.236, bf16[1184,12,64]{0,2,1:T(8,128)(2,1)} %bitcast.219), kind=kOutput, calls=%fused_computation.244 | convolution fusion | flops 480117920 | bytes 2225312 | tf_op jit(solution)/shard_map/sub | solution.py:40
  468.4 9.3 %fusion.91 = bf16[12,64,256]{2,1,0:T(8,128)(2,1)} fusion(bf16[1184,12,64]{0,2,1:T(8,128)(2,1)} %bitcast.226, f32[12,256]{1,0:T(8,128)S(1)} %fusion.179, pred[1184]{0:T(1024)(128)(4,1)S(1)} %copy-done.28, bf16[256,12,64]{0,2,1:T(8,128)(2,1)S(1)} %bitcast.237, bf16[1184,12,64]{0,2,1:T(8,128)(2,1)} %bitcast.220), kind=kOutput, calls=%fused_computation.129 | convolution fusion | flops 949522560 | bytes 4437152 | tf_op jit(solution)/shard_map/hqk,khd->qhd/dot_general | solution.py:42
  477.7 2.1 fusion.36
  482.4 3.1 collective-permute-start.1
  485.8 2.7 maximum_select_fusion
  488.5 1.6 multiply_add_fusion
  (120 shorter events, 22.0 us)
Async XLA Ops:
  7.2 149.3 %all-gather.11.cloned.1.call-start = ((), (), s32[]{:S(2)}) async-start(), calls=%async_computation.2 | async-start | bytes 14266368 | tf_op jit(solution)/shard_map/all_gather | solution.py:61
  8.8 263.1 %all-gather.13.cloned.1.call-start = ((), (), s32[]{:S(2)}) async-start(), calls=%async_computation.3 | async-start | bytes 4755456 | tf_op jit(solution)/shard_map/all_gather | solution.py:62
  10.3 306.1 %all-gather.7.cloned.1.call-start = ((), (), s32[]{:S(2)}) async-start(), calls=%async_computation | async-start | bytes 3932160 | tf_op jit(solution)/shard_map/all_gather | solution.py:84
  15.7 149.7 %copy-start.23 = (bf16[1,2,24,1536]{3,2,1,0:T(8,128)(2,1)S(1)}, bf16[1,2,24,1536]{3,2,1,0:T(8,128)(2,1)}, u32[]{:S(2)}) copy-start(bf16[1,2,24,1536]{3,2,1,0:T(8,128)(2,1)} %param.17) | copy-start | bytes 442372
  169.7 0.9 copy-start.13
  170.6 189.7 %all-gather.9.cloned.1.call-start = ((), (), s32[]{:S(2)}) async-start(), calls=%async_computation.1 | async-start | bytes 3932160 | tf_op jit(solution)/shard_map/all_gather | solution.py:84
  173.9 2.6 copy-start.31
  173.9 4.5 copy-start
  175.6 0.9 copy-start.12
  177.8 204.5 %copy-start.27 = (pred[1184]{0:T(1024)(128)(4,1)}, pred[1184]{0:T(1024)(128)(4,1)S(1)}, u32[]{:S(2)}) copy-start(pred[1184]{0:T(1024)(128)(4,1)S(1)} %concatenate.35) | copy-start | bytes 3556
  178.4 220.5 %copy-start.29 = (pred[1184]{0:T(1024)(128)(4,1)}, pred[1184]{0:T(1024)(128)(4,1)S(1)}, u32[]{:S(2)}) copy-start(pred[1184]{0:T(1024)(128)(4,1)S(1)} %concatenate.37) | copy-start | bytes 3556
  271.9 3.0 copy-start.1
  280.2 1.0 copy-start.21
  289.6 1.0 copy-start.19
  316.4 3.9 copy-start.6
  316.4 3.9 copy-start.22
  360.4 3.9 copy-start.7
  360.4 3.9 copy-start.20
  408.3 2.2 copy-start.2
  408.3 10.9 %slice-start = ((s8[7077888]{0:T(1024)(128)(4,1)}), s8[4194304]{0:T(1024)(128)(4,1)S(1)}, s32[]{:S(2)}) async-start(s8[7077888]{0:T(1024)(128)(4,1)} %bitcast.212), calls=%async_computation.4 | async-start | bytes 8388608
  410.5 8.7 %slice-start.1 = ((s8[7077888]{0:T(1024)(128)(4,1)}), s8[2883584]{0:T(1024)(128)(4,1)S(1)}, s32[]{:S(2)}) async-start(s8[7077888]{0:T(1024)(128)(4,1)} %bitcast.212), calls=%async_computation.5 | async-start | bytes 5767168
  413.0 5.3 %collective-permute-start = (bf16[2,256,1536]{2,1,0:T(8,128)(2,1)S(1)}, bf16[2,256,1536]{2,1,0:T(8,128)(2,1)S(1)}, u32[]{:S(2)}, u32[]{:S(2)}) collective-permute-start(bf16[2,256,1536]{2,1,0:T(8,128)(2,1)S(1)} %pad_maximum_fusion.4), channel_id=1, source_target_pairs={{0,128},{1,129},{2,130},{3,131},{4,132},{5,133},{6,134},{7,135},{8... | collective-permute-start | bytes 4718600 | tf_op jit(solution)/shard_map/ppermute | solution.py:16
  418.3 4.4 copy-start.4
  419.2 2.2 copy-start.9
  421.4 1.3 copy-start.17
  422.7 2.2 copy-start.8
  424.9 4.6 copy-start.18
  429.5 4.0 slice-start.2
  433.7 12.3 %copy-start.25 = (bf16[256,768]{0,1:T(8,128)(2,1)}, bf16[256,768]{0,1:T(8,128)(2,1)S(1)}, u32[]{:S(2)}) copy-start(bf16[256,768]{0,1:T(8,128)(2,1)S(1)} %copy.62) | copy-start | bytes 1179652
  437.7 4.0 slice-start.3
  441.9 4.1 copy-start.30
  452.7 8.7 %copy-start.28 = (pred[1184]{0:T(1024)(128)(4,1)S(1)}, pred[1184]{0:T(1024)(128)(4,1)}, u32[]{:S(2)}) copy-start(pred[1184]{0:T(1024)(128)(4,1)} %copy-done.27) | copy-start | bytes 3556
  477.7 2.1 copy-start.5
  477.7 2.1 copy-start.24
  480.6 0.9 copy-start.10
  481.5 4.1 copy-start.26
  481.5 4.2 copy-start.14
  481.5 4.2 copy-start.15
  481.5 4.3 copy-start.16
  482.4 6.0 %collective-permute-start.1 = (bf16[2,256,768]{2,1,0:T(8,128)(2,1)}, bf16[2,256,768]{2,1,0:T(8,128)(2,1)}, u32[]{:S(2)}, u32[]{:S(2)}) collective-permute-start(bf16[2,256,768]{2,1,0:T(8,128)(2,1)} %fusion.94), channel_id=1, source_target_pairs={{128,0},{129,1},{130,2},{131,3},{132,4},{133,5},{134,6},{135,7},{1... | collective-permute-start | bytes 2359304 | tf_op jit(solution)/shard_map/ppermute | solution.py:16
  485.7 2.7 copy-start.3
  485.7 2.7 copy-start.11
Sparse Core Ops, SparseCore 0:
  12.3 144.0 all-gather.10
  160.8 111.1 all-gather.12
  273.7 42.6 all-gather.6
  318.1 42.2 all-gather.8
where the time goes:
time: 502 us; the launch traced here: 497 us
  waiting for transfers between devices  288 us (57%)
  matrix products  93.5 us (19%)
  local copies, waits for them, and re-layouts  76.1 us (15%)
  other arithmetic  19.8 us (4%)
  between operations  14.6 us (3%)
    all_gather x1, waiting for transfers between devices, body(): lax.all_gather(w_qkv[0], ('patch', 'req'), axis=0, tiled=True)  141 us
    all_gather x1, waiting for transfers between devices, body(): lax.all_gather(w_out[0], ('patch', 'req'), axis=0, tiled=True)  91.4 us
    all_gather x2, waiting for transfers between devices, process(): image_rows = lax.all_gather(patched, 'patch', axis=0, tiled=True)  52.2 us
    dot_general x4, matrix products, attend(): jnp.einsum('hqk,khd->qhd', soft_weights, value_heads, preferred_element_t...  36.9 us
    unnamed x74, local copies, waits for them, and re-layouts  27.8 us
    sub x4, matrix products, attend(): exp_scores = jnp.exp(scores - row_max)  27.6 us
    slice x4, local copies, waits for them, and re-layouts, process(): context[:, head_width:]  16.2 us
    slice x4, local copies, waits for them, and re-layouts, process(): context[:, :head_width]  15.8 us
  transfers between devices with their start and end apart: 6, of which 5 were waited for; matrix products, arithmetic and copies ran while one was open for 13% of the time, Pallas kernels for 0%

commit v1 on v0

v1 whole, which is shorter than its diff:
```python
import jax
import jax.numpy as jnp
from jax import lax
from jax.sharding import PartitionSpec as P

HEADS = 12


norm_eps = 1e-06
score_scale = 0.125


def shifted(block, axis, distance):
    devices = range(lax.axis_size(axis))
    route = [(i - distance, i) for i in devices if i - distance in devices]
    return lax.ppermute(block, axis, route)


def rotated(block, axis, distance):
    size = lax.axis_size(axis)
    return lax.ppermute(block, axis, [(i, (i + distance) % size) for i in range(size)])


def modulate(row_block, shift_row, scale_row):
    values = row_block.astype(jnp.float32)
    centre = values - jnp.mean(values, axis=-1, keepdims=True)
    spread = jnp.mean(centre * centre, axis=-1, keepdims=True)
    return (centre * lax.rsqrt(spread + norm_eps) * (1.0 + scale_row) + shift_row).astype(
        jnp.bfloat16
    )


def attend(queries, key_rows, value_rows, usable):
    row_count = queries.shape[0]
    feature_count = queries.shape[1]
    query_heads = queries.reshape(row_count, HEADS, feature_count // HEADS)
    key_heads = key_rows.reshape(key_rows.shape[0], HEADS, feature_count // HEADS)
    value_heads = value_rows.reshape(value_rows.shape[0], HEADS, feature_count // HEADS)
    scores = (
        jnp.einsum("qhd,khd->hqk", query_heads, key_heads, preferred_element_type=jnp.float32)
        * score_scale
    )
    scores = jnp.where(usable[None, None, :], scores, -1e30)
    row_max = jnp.max(scores, axis=-1, keepdims=True)
    exp_scores = jnp.exp(scores - row_max)
    soft_weights = (exp_scores / jnp.sum(exp_scores, axis=-1, keepdims=True)).astype(jnp.bfloat16)
    attended = jnp.einsum(
        "hqk,khd->qhd", soft_weights, value_heads, preferred_element_type=jnp.float32
    )
    return attended.reshape(row_count, feature_count).astype(jnp.bfloat16)


def gather_weights(w_qkv, w_out):
    qkv_shard = w_qkv[0]
    out_shard = w_out[0]
    qkv_rows, qkv_cols = qkv_shard.shape
    out_rows, out_cols = out_shard.shape
    flat = jnp.concatenate([qkv_shard.reshape(-1), out_shard.reshape(-1)]).reshape(-1, 128)
    gathered = lax.all_gather(flat, "patch", axis=0, tiled=True)
    gathered = lax.all_gather(gathered, "req", axis=0, tiled=True)
    patches = lax.axis_size("patch")
    requests = lax.axis_size("req")
    gathered = gathered.reshape(requests, patches, -1).transpose(1, 0, 2)
    gathered = gathered.reshape(patches * requests, -1)
    qkv_size = qkv_rows * qkv_cols
    full_qkv = gathered[:, :qkv_size].reshape(-1, qkv_cols)
    full_out = gathered[:, qkv_size:].reshape(-1, out_cols)
    return full_qkv, full_out


def body(
    hidden,
    w_qkv,
    w_out,
    modulation,
    text_kv,
    text_lengths,
    stale_kv,
    held_hidden,
    recompute_rows,
    coefficients,
):
    section_index = lax.axis_index("section")
    patch_count = lax.axis_size("patch")
    request_count = hidden.shape[0]
    patch_rows = hidden.shape[1]
    model_width = hidden.shape[2]
    held_count = held_hidden.shape[2]
    text_slots = text_kv.shape[2]

    index_row = jnp.zeros((request_count, 1, model_width), jnp.bfloat16)
    index_row = index_row.at[:, 0, :held_count].set(recompute_rows[0].astype(jnp.bfloat16))
    payload = jnp.concatenate([stale_kv[0], held_hidden[0], index_row], axis=1)
    arrivals = [rotated(payload, "patch", distance) for distance in range(1, patch_count)]

    full_qkv, full_out = gather_weights(w_qkv, w_out)
    head_width = full_out.shape[0]
    key_weights = full_qkv[:, head_width:]

    others = []
    for slot in range(request_count):
        mod_rows = modulation[0, slot]
        pieces = []
        for arrival in arrivals:
            stale_rows = arrival[slot, :patch_rows]
            held_rows = arrival[slot, patch_rows : patch_rows + held_count]
            redo_index = arrival[slot, patch_rows + held_count, :held_count].astype(jnp.int32)
            held_norm = modulate(held_rows, mod_rows[0], mod_rows[1])
            redone = jnp.dot(held_norm, key_weights, preferred_element_type=jnp.float32).astype(
                jnp.bfloat16
            )
            pieces.append(stale_rows.at[redo_index].set(redone))
        others.append(jnp.concatenate(pieces, axis=0))
    others = jnp.stack(others)

    def process(layer_input, slot_index):
        mod_rows = lax.dynamic_index_in_dim(modulation[0], slot_index, 0, keepdims=False)
        text_rows = lax.dynamic_index_in_dim(text_kv[0], slot_index, 0, keepdims=False)
        text_count = lax.dynamic_index_in_dim(text_lengths, slot_index, 0, keepdims=False)
        other_rows = lax.dynamic_index_in_dim(others, slot_index, 0, keepdims=False)
        normed = modulate(layer_input, mod_rows[0], mod_rows[1])
        projected = jnp.dot(normed, full_qkv, preferred_element_type=jnp.float32).astype(
            jnp.bfloat16
        )
        fresh_rows = projected[:, head_width:]
        context = jnp.concatenate([text_rows, fresh_rows, other_rows], axis=0)
        usable = jnp.concatenate(
            [
                jnp.arange(text_slots) < text_count,
                jnp.ones((context.shape[0] - text_slots,), jnp.bool_),
            ]
        )
        attended = attend(
            projected[:, :head_width], context[:, :head_width], context[:, head_width:], usable
        )
        update = jnp.dot(attended, full_out, preferred_element_type=jnp.float32)
        layer_out = (layer_input.astype(jnp.float32) + mod_rows[2] * update).astype(jnp.bfloat16)
        return layer_out, fresh_rows

    first_section = section_index == 0
    half_width = model_width // 2

    out_1, fresh_1 = process(hidden[0], 0)
    received_1 = shifted(out_1, "section", 1)
    input_2 = jnp.where(first_section, hidden[1], received_1)
    out_2, fresh_2 = process(input_2, jnp.where(first_section, 1, 0))
    returned_a = shifted(out_2[:, :half_width], "section", -1)
    received_2 = shifted(out_2, "section", 1)
    out_3, fresh_3 = process(received_2, 1)
    returned_b = shifted(out_3[:, :half_width], "section", -1)

    cache = jnp.stack(
        [jnp.where(first_section, fresh_1, fresh_2), jnp.where(first_section, fresh_2, fresh_3)]
    )
    last_out = jnp.stack([out_2, out_3])
    returned = jnp.stack([returned_a, returned_b])
    own_half = jnp.where(first_section, returned, last_out[:, :, half_width:])
    source_half = lax.dynamic_slice_in_dim(hidden, section_index * half_width, half_width, 2)
    latents = coefficients[:, 0][:, None, None] * source_half.astype(jnp.float32) + coefficients[
        :, 1
    ][:, None, None] * own_half.astype(jnp.float32)
    return (latents, cache[None])


def solution(mesh):
    return jax.shard_map(
        body,
        mesh=mesh,
        in_specs=(
            P("req", "patch", None),
            P("section", ("patch", "req"), None),
            P("section", ("patch", "req"), None),
            P("section", "req", None, None),
            P("section", "req", None, None),
            P("req"),
            P("section", "req", "patch", None),
            P("section", "req", "patch", None),
            P("section", "req", "patch"),
            P("req", None),
        ),
        out_specs=(P("req", "patch", "section"), P("section", "req", "patch", None)),
        check_vma=False,
    )
```

time: 502 us -> 375 us (0.75)
  waiting for transfers between devices: 288 us -> 66.9 us
  local copies, waits for them, and re-layouts: 76.1 us -> 154 us
  matrix products: 93.5 us -> 80.3 us
  blocking collectives: 0 us -> 12 us
  other arithmetic: 19.8 us -> 28.7 us
  starting transfers between devices: 4.55 us -> 11 us
    all_gather x4 -> x1, waiting for transfers between devices: 284 us -> 12.8 us  [gather_weights(): gathered = lax.all_gather(gathered, 'req', axis=0, tiled=True)]
    ppermute x0 -> x3, waiting for transfers between devices: none -> 54 us  [rotated(): lax.ppermute(block, axis, [(i, (i + distance) % size) for i in range(size)])]
    reshape x0 -> x3, local copies, waits for them, and re-layouts: none -> 31.6 us  [the longest x1 13.7 us: gather_weights(): full_qkv = gathered[:, :qkv_size].reshape(-1, qkv_cols)]
    slice x0 -> x9, local copies, waits for them, and re-layouts: none -> 24.8 us  [the longest x3 11.1 us: body(): stale_rows = arrival[slot, :patch_rows]]
    scatter x2 -> x6, local copies, waits for them, and re-layouts: 2.87 us -> 16.5 us  [body(): pieces.append(stale_rows.at[redo_index].set(redone))]
    transpose x0 -> x1, local copies, waits for them, and re-layouts: none -> 12.5 us  [gather_weights(): gathered = gathered.reshape(requests, patches, -1).transpose(1, 0, 2)]
    all_gather x0 -> x1, blocking collectives: none -> 12 us  [gather_weights(): gathered = lax.all_gather(flat, 'patch', axis=0, tiled=True)]
    dot_general x4 -> x3, matrix products: 36.9 us -> 26.1 us  [attend(): jnp.einsum('hqk,khd->qhd', soft_weights, value_heads, preferred_element_t...]
  transfers between devices with their start and end apart: 6 -> 8, of which waited for: 5 -> 3; matrix products, arithmetic and copies ran while one was open for 13% -> 26% of each run, Pallas kernels for 0% -> 0%
where the time goes in v1:
time: 375 us; the launch traced here: 368 us
  local copies, waits for them, and re-layouts  154 us (41%)
  matrix products  80.3 us (21%)
  waiting for transfers between devices  66.9 us (18%)
  other arithmetic  28.7 us (8%)
  between operations  14.9 us (4%)
  blocking collectives  12 us (3%)
  starting transfers between devices  11 us (3%)
    ppermute x3, waiting for transfers between devices, rotated(): lax.ppermute(block, axis, [(i, (i + distance) % size) for i in range(size)])  54 us
    dot_general x3, matrix products, attend(): jnp.einsum('hqk,khd->qhd', soft_weights, value_heads, preferred_element_t...  26.1 us
    slice x6, local copies, waits for them, and re-layouts, process(): context[:, :head_width]  22.1 us
    sub x3, matrix products, attend(): exp_scores = jnp.exp(scores - row_max)  22 us
    unnamed x96, local copies, waits for them, and re-layouts  21.6 us
    scatter x6, local copies, waits for them, and re-layouts, body(): pieces.append(stale_rows.at[redo_index].set(redone))  16.5 us
    reshape x1, local copies, waits for them, and re-layouts, gather_weights(): full_qkv = gathered[:, :qkv_size].reshape(-1, qkv_cols)  13.7 us
    reshape x1, local copies, waits for them, and re-layouts, gather_weights(): gathered = gathered.reshape(requests, patches, -1).transpose(1, 0, 2)  13.6 us
  transfers between devices with their start and end apart: 8, of which 3 were waited for; matrix products, arithmetic and copies ran while one was open for 26% of the time, Pallas kernels for 0%

profile of v1, /device:TPU:1, one launch (start us, length us, event | category | flops | bytes accessed | tf_op | source)
XLA Modules:
  0.0 368.0 jit_solution(17884248741087096478)
XLA Ops:
  9.0 12.0 %all_gather.6 = bf16[1152,128]{1,0:T(8,128)(2,1)} all-gather(bf16[288,128]{1,0:T(8,128)(2,1)S(1)} %maximum_bitcast_fusion.3), channel_id=1, replica_groups=mesh['section'=2,'patch'=4,'req'=32] {'patch'}, dimensions={0}, use_global_device_ids=true | all-gather | bytes 368640 | tf_op jit(solution)/shard_map/all_gather | solution.py:59
  22.1 3.0 copy.120
  25.2 2.9 fusion.43
  37.6 26.3 %collective-permute-done.2 = bf16[2,281,1536]{2,0,1:T(2,128)(2,1)} collective-permute-done((bf16[2,281,1536]{2,0,1:T(2,128)(2,1)}, bf16[2,281,1536]{2,0,1:T(2,128)(2,1)}, u32[]{:S(2)}, u32[]{:S(2)}) %collective-permute-start.2) | collective-permute-done | bytes 1726496 | tf_op jit(solution)/shard_map/ppermute | solution.py:21
  63.9 4.5 %fusion.182 = (bf16[1,256,1536]{2,0,1:T(2,128)(2,1)S(1)}, bf16[1,256,1536]{2,0,1:T(2,128)(2,1)S(1)}) fusion(bf16[2,281,1536]{2,0,1:T(2,128)(2,1)} %collective-permute-done.2), kind=kLoop, calls=%fused_computation.293 | loop fusion | bytes 3145728 | tf_op jit(solution)/shard_map/slice | solution.py:105
  70.4 4.3 %fusion.180 = (bf16[1,256,1536]{2,0,1:T(2,128)(2,1)S(1)}, bf16[1,256,1536]{2,0,1:T(2,128)(2,1)S(1)}) fusion(bf16[2,281,1536]{2,0,1:T(2,128)(2,1)} %collective-permute-done.1), kind=kLoop, calls=%fused_computation.291 | loop fusion | bytes 3145728 | tf_op jit(solution)/shard_map/slice | solution.py:105
  80.5 27.7 %collective-permute-done = bf16[2,281,1536]{2,0,1:T(2,128)(2,1)S(1)} collective-permute-done((bf16[2,281,1536]{2,0,1:T(2,128)(2,1)}, bf16[2,281,1536]{2,0,1:T(2,128)(2,1)S(1)}, u32[]{:S(2)}, u32[]{:S(2)}) %collective-permute-start) | collective-permute-done | bytes 1726496 | tf_op jit(solution)/shard_map/ppermute | solution.py:21
  112.4 2.2 fusion.178
  115.8 12.8 %all-gather.2.cloned.1.call-done = bf16[36864,128]{1,0:T(8,128)(2,1)} async-done(((bf16[1152,128]{1,0:T(8,128)(2,1)}), bf16[36864,128]{1,0:T(8,128)(2,1)}) %all-gather.2.cloned.1.call-update) | async-done | bytes 9437200 | tf_op jit(solution)/shard_map/all_gather | solution.py:60
  128.7 13.6 %reshape.439 = bf16[32,4,36864]{2,1,0:T(4,128)(2,1)} reshape(bf16[36864,128]{1,0:T(8,128)(2,1)} %all-gather.2.cloned.1.call-done) | data formatting | bytes 18874368 | tf_op jit(solution)/shard_map/reshape | solution.py:63
  142.3 12.5 %copy.42 = bf16[4,32,36864]{2,1,0:T(8,128)(2,1)} copy(bf16[4,32,36864]{2,0,1:T(4,128)(2,1)} %bitcast.255) | data formatting | bytes 18874368 | tf_op jit(solution)/shard_map/transpose | solution.py:63
  154.7 3.2 slice.279
  158.0 6.3 %slice.264 = bf16[128,27648]{1,0:T(8,128)(2,1)} slice(bf16[128,36864]{1,0:T(8,128)(2,1)} %bitcast.254), slice={[0:128], [0:27648]} | slice | bytes 14155776 | tf_op jit(solution)/shard_map/slice | solution.py:66
  164.3 13.7 %reshape.441 = bf16[1536,2304]{1,0:T(8,128)(2,1)} reshape(bf16[128,27648]{1,0:T(8,128)(2,1)} %slice.264) | data formatting | bytes 14155776 | tf_op jit(solution)/shard_map/reshape | solution.py:66
  178.0 3.9 %convolution_convert_fusion.7 = bf16[24,1536]{1,0:T(8,128)(2,1)} fusion(bf16[1536,2304]{1,0:T(8,128)(2,1)} %reshape.441, f32[24]{0:T(128)S(1)} %add_rsqrt_fusion.7, f32[24]{0:T(128)S(1)} %broadcast_multiply_fusion.7, f32[1536]{0:T(1024)S(1)} %get-tuple-element.21, f32[1536]{0:T(1024)S(1)} %get-tuple-element.22, bf16[1,24,1536]{2,0,1:T(2,128)(2,1)S(1)} %get-tuple-element.42), kind=kOutput, calls=%fused_computation.67 | convolution fusion | flops 113504256 | bytes 4878528 | tf_op jit(solution)/shard_map/dot_general | solution.py:109
  181.9 3.8 %convolution_convert_fusion.6 = bf16[24,1536]{1,0:T(8,128)(2,1)} fusion(bf16[1536,2304]{1,0:T(8,128)(2,1)} %reshape.441, f32[24]{0:T(128)S(1)} %add_rsqrt_fusion.6, f32[24]{0:T(128)S(1)} %broadcast_multiply_fusion.6, f32[1536]{0:T(1024)S(1)} %get-tuple-element.21, f32[1536]{0:T(1024)S(1)} %get-tuple-element.22, bf16[1,24,1536]{2,0,1:T(2,128)(2,1)S(1)} %get-tuple-element.48), kind=kOutput, calls=%fused_computation.66 | convolution fusion | flops 113504256 | bytes 4878528 | tf_op jit(solution)/shard_map/dot_general | solution.py:109
  191.4 4.3 %reshape.445 = bf16[768,1536]{1,0:T(8,128)(2,1)S(1)} reshape(bf16[128,9216]{1,0:T(8,128)(2,1)} %slice.279) | data formatting | bytes 4718592 | tf_op jit(solution)/shard_map/reshape | solution.py:67
  195.7 5.4 %convolution_convert_fusion.2 = bf16[256,2304]{1,0:T(8,128)(2,1)S(1)} fusion(bf16[1536,2304]{1,0:T(8,128)(2,1)} %reshape.441, f32[1536]{0:T(1024)S(1)} %get-tuple-element.21, f32[1536]{0:T(1024)S(1)} %get-tuple-element.22, f32[256]{0:T(256)S(1)} %add_rsqrt_fusion.2, f32[256]{0:T(256)S(1)} %broadcast_multiply_fusion.2, bf16[2,256,1536]{2,1,0:T(8,128)(2,1)} %param.12), kind=kOutput, calls=%fused_computation.38 | convolution fusion | flops 1814888448 | bytes 9058304 | tf_op jit(solution)/shard_map/dot_general | solution.py:122
  205.3 3.2 scatter_fusion
  210.6 2.8 scatter_fusion.1
  213.4 2.1 constant_dynamic-update-slice_fusion.1
  215.5 2.8 scatter_fusion.2
  218.4 2.1 constant_dynamic-update-slice_fusion
  220.5 4.1 %fusion.177 = (bf16[1184,768]{1,0:T(8,128)(2,1)}, bf16[1184,768]{1,0:T(8,128)(2,1)}) fusion(bf16[1184,1536]{1,0:T(8,128)(2,1)} %constant_dynamic-update-slice_fusion), kind=kLoop, calls=%fused_computation.288 | loop fusion | bytes 7274496 | tf_op jit(solution)/shard_map/slice | solution.py:134
  224.6 4.0 %copy.52 = bf16[1184,768]{0,1:T(8,128)(2,1)} copy(bf16[1184,768]{1,0:T(8,128)(2,1)} %get-tuple-element.33) | data formatting | bytes 3637248 | tf_op jit(solution)/shard_map/slice | solution.py:134
  228.6 4.2 %copy.50 = bf16[1184,768]{0,1:T(8,128)(2,1)} copy(bf16[1184,768]{1,0:T(8,128)(2,1)} %get-tuple-element.34) | data formatting | bytes 3637248 | tf_op jit(solution)/shard_map/slice | solution.py:134
  232.7 7.3 %fusion.184 = f32[12,256]{1,0:T(8,128)} fusion(pred[1184]{0:T(1024)(128)(4,1)} %concatenate.37, bf16[256,12,64]{0,2,1:T(8,128)(2,1)S(1)} %bitcast.280, bf16[1184,12,64]{0,2,1:T(8,128)(2,1)} %bitcast.265), kind=kOutput, calls=%fused_computation.295 | convolution fusion | flops 480117920 | bytes 2225312 | tf_op jit(solution)/shard_map/sub | solution.py:45
  240.1 8.7 %fusion.60 = bf16[12,64,256]{2,1,0:T(8,128)(2,1)S(1)} fusion(bf16[1184,12,64]{0,2,1:T(8,128)(2,1)} %bitcast.271, f32[12,256]{1,0:T(8,128)} %fusion.184, pred[1184]{0:T(1024)(128)(4,1)} %concatenate.37, bf16[256,12,64]{0,2,1:T(8,128)(2,1)} %bitcast.279, bf16[1184,12,64]{0,2,1:T(8,128)(2,1)} %bitcast.266), kind=kOutput, calls=%fused_computation.100 | convolution fusion | flops 949522560 | bytes 4437152 | tf_op jit(solution)/shard_map/hqk,khd->qhd/dot_general | solution.py:47
  248.8 3.2 fusion.21
  253.4 3.2 scatter_fusion.5
  256.6 3.2 scatter_fusion.4
  263.3 2.3 fusion.25
  265.6 2.2 convert_reduce_fusion.1
  268.3 2.2 convolution_convert_fusion.1
  273.7 2.1 pad_maximum_fusion
  277.8 4.0 %copy.60 = bf16[1184,768]{0,1:T(8,128)(2,1)} copy(bf16[1184,768]{1,0:T(8,128)(2,1)} %get-tuple-element.31) | data formatting | bytes 3637248 | tf_op jit(solution)/shard_map/slice | solution.py:134
  281.8 4.0 %copy.58 = bf16[1184,768]{0,1:T(8,128)(2,1)} copy(bf16[1184,768]{1,0:T(8,128)(2,1)} %get-tuple-element.32) | data formatting | bytes 3637248 | tf_op jit(solution)/shard_map/slice | solution.py:134
  285.8 7.3 %fusion.185 = f32[12,256]{1,0:T(8,128)} fusion(pred[1184]{0:T(1024)(128)(4,1)S(1)} %copy-done.38, bf16[256,12,64]{0,2,1:T(8,128)(2,1)S(1)} %bitcast.284, bf16[1184,12,64]{0,2,1:T(8,128)(2,1)} %bitcast.267), kind=kOutput, calls=%fused_computation.296 | convolution fusion | flops 480117920 | bytes 2225312 | tf_op jit(solution)/shard_map/sub | solution.py:45
  293.2 8.7 %fusion.59 = bf16[12,64,256]{2,1,0:T(8,128)(2,1)S(1)} fusion(bf16[1184,12,64]{0,2,1:T(8,128)(2,1)} %bitcast.272, f32[12,256]{1,0:T(8,128)} %fusion.185, pred[1184]{0:T(1024)(128)(4,1)S(1)} %copy-done.38, bf16[256,12,64]{0,2,1:T(8,128)(2,1)} %bitcast.283, bf16[1184,12,64]{0,2,1:T(8,128)(2,1)} %bitcast.268), kind=kOutput, calls=%fused_computation.99 | convolution fusion | flops 949522560 | bytes 4437152 | tf_op jit(solution)/shard_map/hqk,khd->qhd/dot_general | solution.py:47
  306.5 4.5 %collective-permute-start.4 = (bf16[256,768]{1,0:T(8,128)(2,1)}, bf16[256,768]{1,0:T(8,128)(2,1)}, u32[]{:S(2)}, u32[]{:S(2)}) collective-permute-start(bf16[256,768]{1,0:T(8,128)(2,1)} %slice.293), channel_id=1, source_target_pairs={{128,0},{129,1},{130,2},{131,3},{132,4},{133,5},{134,6},{135,7},{1... | collective-permute-start | bytes 1179656 | tf_op jit(solution)/shard_map/ppermute | solution.py:16
  311.7 5.3 %convolution_convert_fusion = bf16[256,2304]{1,0:T(8,128)(2,1)S(1)} fusion(bf16[1536,2304]{1,0:T(8,128)(2,1)} %reshape.441, bf16[256,1536]{1,0:T(8,128)(2,1)S(1)} %collective-permute-done.5, f32[1536]{0:T(1024)S(1)} %copy-done.30, f32[1536]{0:T(1024)S(1)} %copy-done.28, f32[256]{0:T(256)S(1)} %add_rsqrt_fusion, f32[256]{0:T(256)S(1)} %broadcast_multiply_fusion), kind=kOutput, calls=%fused_computation.36 | convolution fusion | flops 1814888448 | bytes 9058304 | tf_op jit(solution)/shard_map/dot_general | solution.py:122
  323.3 4.1 %fusion.175 = (bf16[1184,768]{1,0:T(8,128)(2,1)}, bf16[1184,768]{1,0:T(8,128)(2,1)}) fusion(bf16[1184,1536]{1,0:T(8,128)(2,1)} %constant_dynamic-update-slice_fusion.3), kind=kLoop, calls=%fused_computation.286 | loop fusion | bytes 7274496 | tf_op jit(solution)/shard_map/slice | solution.py:134
  327.4 3.9 %copy.63 = bf16[1184,768]{0,1:T(8,128)(2,1)} copy(bf16[1184,768]{1,0:T(8,128)(2,1)} %get-tuple-element.29) | data formatting | bytes 3637248 | tf_op jit(solution)/shard_map/slice | solution.py:134
  331.4 4.1 %copy.61 = bf16[1184,768]{0,1:T(8,128)(2,1)} copy(bf16[1184,768]{1,0:T(8,128)(2,1)} %get-tuple-element.30) | data formatting | bytes 3637248 | tf_op jit(solution)/shard_map/slice | solution.py:134
  335.5 7.3 %fusion.186 = f32[12,256]{1,0:T(8,128)} fusion(pred[1184]{0:T(1024)(128)(4,1)S(1)} %concatenate.43, bf16[256,12,64]{0,2,1:T(8,128)(2,1)S(1)} %bitcast.282, bf16[1184,12,64]{0,2,1:T(8,128)(2,1)} %bitcast.269), kind=kOutput, calls=%fused_computation.297 | convolution fusion | flops 480117920 | bytes 2225312 | tf_op jit(solution)/shard_map/sub | solution.py:45
  342.8 8.8 %fusion.58 = bf16[12,64,256]{2,1,0:T(8,128)(2,1)S(1)} fusion(bf16[1184,12,64]{0,2,1:T(8,128)(2,1)} %bitcast.273, f32[12,256]{1,0:T(8,128)} %fusion.186, pred[1184]{0:T(1024)(128)(4,1)S(1)} %concatenate.43, bf16[256,12,64]{0,2,1:T(8,128)(2,1)} %bitcast.281, bf16[1184,12,64]{0,2,1:T(8,128)(2,1)} %bitcast.270), kind=kOutput, calls=%fused_computation.98 | convolution fusion | flops 949522560 | bytes 4437152 | tf_op jit(solution)/shard_map/hqk,khd->qhd/dot_general | solution.py:47
  355.7 2.7 maximum_bitcast_fusion.2
  358.4 2.6 multiply_add_fusion
  (181 shorter events, 63.3 us)
Async XLA Ops:
  7.2 18.0 %copy-start.39 = (s32[1,2,24]{2,1,0:T(2,128)S(1)}, s32[1,2,24]{2,1,0:T(2,128)}, u32[]{:S(2)}) copy-start(s32[1,2,24]{2,1,0:T(2,128)} %param.20) | copy-start | bytes 580
  7.2 121.5 %all-gather.2.cloned.1.call-start = ((), (), s32[]{:S(2)}) async-start(), calls=%async_computation | async-start | bytes 9732096 | tf_op jit(solution)/shard_map/all_gather | solution.py:60
  25.1 5.2 %copy-start.33 = (s32[2]{0:T(128)S(1)}, s32[2]{0:T(128)}, u32[]{:S(2)}) copy-start(s32[2]{0:T(128)} %param.17) | copy-start | bytes 28
  25.1 8.3 %copy-start.3 = (bf16[2,256,1536]{2,1,0:T(8,128)(2,1)S(1)}, bf16[2,256,1536]{2,1,0:T(8,128)(2,1)}, u32[]{:S(2)}) copy-start(bf16[2,256,1536]{2,1,0:T(8,128)(2,1)} %param.12) | copy-start | bytes 4718596
  25.2 8.8 %copy-start.22 = (f32[1,2,3,1536]{3,1,2,0:T(2,128)S(1)}, f32[1,2,3,1536]{3,1,2,0:T(2,128)}, u32[]{:S(2)}) copy-start(f32[1,2,3,1536]{3,1,2,0:T(2,128)} %param.15) | copy-start | bytes 110596
  28.1 35.8 %collective-permute-start.2 = (bf16[2,281,1536]{2,0,1:T(2,128)(2,1)}, bf16[2,281,1536]{2,0,1:T(2,128)(2,1)}, u32[]{:S(2)}, u32[]{:S(2)}) collective-permute-start(bf16[2,281,1536]{2,0,1:T(2,128)(2,1)} %fusion.43), channel_id=1, source_target_pairs={{0,96},{32,0},{64,32},{96,64},{1,97},{33,1},{65,33},{97,65},{2,98}... | collective-permute-start | bytes 5179400 | tf_op jit(solution)/shard_map/ppermute | solution.py:21
  29.8 40.7 %collective-permute-start.1 = (bf16[2,281,1536]{2,0,1:T(2,128)(2,1)}, bf16[2,281,1536]{2,0,1:T(2,128)(2,1)}, u32[]{:S(2)}, u32[]{:S(2)}) collective-permute-start(bf16[2,281,1536]{2,0,1:T(2,128)(2,1)} %fusion.43), channel_id=1, source_target_pairs={{0,64},{32,96},{64,0},{96,32},{1,65},{33,97},{65,1},{97,33},{2,66}... | collective-permute-start | bytes 5179400 | tf_op jit(solution)/shard_map/ppermute | solution.py:21
  30.3 77.8 %collective-permute-start = (bf16[2,281,1536]{2,0,1:T(2,128)(2,1)}, bf16[2,281,1536]{2,0,1:T(2,128)(2,1)S(1)}, u32[]{:S(2)}, u32[]{:S(2)}) collective-permute-start(bf16[2,281,1536]{2,0,1:T(2,128)(2,1)} %fusion.43), channel_id=1, source_target_pairs={{0,32},{32,64},{64,96},{96,0},{1,33},{33,65},{65,97},{97,1},{2,34}... | collective-permute-start | bytes 5179400 | tf_op jit(solution)/shard_map/ppermute | solution.py:21
  30.4 6.2 %copy-start.18 = (bf16[1,2,160,1536]{3,2,1,0:T(8,128)(2,1)S(1)}, bf16[1,2,160,1536]{3,2,1,0:T(8,128)(2,1)}, u32[]{:S(2)}) copy-start(bf16[1,2,160,1536]{3,2,1,0:T(8,128)(2,1)} %param.16) | copy-start | bytes 2949124
  34.7 153.9 %copy-start.27 = (f32[1536]{0:T(1024)}, f32[1536]{0:T(1024)S(1)}, u32[]{:S(2)}) copy-start(f32[1536]{0:T(1024)S(1)} %get-tuple-element.19) | copy-start | bytes 18436
  34.7 153.9 %copy-start.29 = (f32[1536]{0:T(1024)}, f32[1536]{0:T(1024)S(1)}, u32[]{:S(2)}) copy-start(f32[1536]{0:T(1024)S(1)} %get-tuple-element.24) | copy-start | bytes 18436
  178.0 7.7 %copy-start.6 = (bf16[1536,2304]{1,0:T(8,128)(2,1)S(1)}, bf16[1536,2304]{1,0:T(8,128)(2,1)}, u32[]{:S(2)}) copy-start(bf16[1536,2304]{1,0:T(8,128)(2,1)} %reshape.441) | copy-start | bytes 21233668
  201.1 1.0 copy-start.14
  203.1 7.4 %copy-start.26 = (bf16[24,1536]{1,0:T(8,128)(2,1)S(1)}, bf16[24,1536]{1,0:T(8,128)(2,1)}, u32[]{:S(2)}) copy-start(bf16[24,1536]{1,0:T(8,128)(2,1)} %convolution_convert_fusion.7) | copy-start | bytes 221188
  203.1 7.4 %copy-start.37 = (s32[24]{0:T(128)S(1)}, s32[24]{0:T(128)}, u32[]{:S(2)}) copy-start(s32[24]{0:T(128)} %get-tuple-element.44) | copy-start | bytes 292
  208.5 7.1 %copy-start.25 = (bf16[24,1536]{1,0:T(8,128)(2,1)S(1)}, bf16[24,1536]{1,0:T(8,128)(2,1)}, u32[]{:S(2)}) copy-start(bf16[24,1536]{1,0:T(8,128)(2,1)} %convolution_convert_fusion.6) | copy-start | bytes 221188
  208.5 7.1 %copy-start.36 = (s32[24]{0:T(128)S(1)}, s32[24]{0:T(128)}, u32[]{:S(2)}) copy-start(s32[24]{0:T(128)} %get-tuple-element.50) | copy-start | bytes 292
  228.6 4.2 %copy-start.19 = (bf16[256,768]{0,1:T(8,128)(2,1)S(1)}, bf16[256,768]{0,1:T(8,128)(2,1)}, u32[]{:S(2)}) copy-start(bf16[256,768]{0,1:T(8,128)(2,1)} %copy.51) | copy-start | bytes 1179652
  252.0 7.8 %copy-start.24 = (bf16[24,1536]{1,0:T(8,128)(2,1)S(1)}, bf16[24,1536]{1,0:T(8,128)(2,1)}, u32[]{:S(2)}) copy-start(bf16[24,1536]{1,0:T(8,128)(2,1)} %convolution_convert_fusion.5) | copy-start | bytes 221188
  252.0 7.8 %copy-start.35 = (s32[24]{0:T(128)S(1)}, s32[24]{0:T(128)}, u32[]{:S(2)}) copy-start(s32[24]{0:T(128)} %get-tuple-element.37) | copy-start | bytes 292
  252.0 13.6 %collective-permute-start.3 = (bf16[256,1536]{1,0:T(8,128)(2,1)}, bf16[256,1536]{1,0:T(8,128)(2,1)}, u32[]{:S(2)}, u32[]{:S(2)}) collective-permute-start(bf16[256,1536]{1,0:T(8,128)(2,1)} %fusion.21), channel_id=1, source_target_pairs={{0,128},{1,129},{2,130},{3,131},{4,132},{5,133},{6,134},{7,135},{8... | collective-permute-start | bytes 2359304 | tf_op jit(solution)/shard_map/ppermute | solution.py:16
  261.0 1.9 copy-start
  261.0 2.1 copy-start.2
  263.1 5.1 %slice-start = ((s8[7077888]{0:T(1024)(128)(4,1)}), s8[4194304]{0:T(1024)(128)(4,1)S(1)}, s32[]{:S(2)}) async-start(s8[7077888]{0:T(1024)(128)(4,1)} %bitcast.260), calls=%async_computation.1 | async-start | bytes 8388608
  263.3 2.3 copy-start.4
  263.3 5.0 %slice-start.1 = ((s8[7077888]{0:T(1024)(128)(4,1)}), s8[2883584]{0:T(1024)(128)(4,1)S(1)}, s32[]{:S(2)}) async-start(s8[7077888]{0:T(1024)(128)(4,1)} %bitcast.260), calls=%async_computation.2 | async-start | bytes 5767168
  265.6 2.6 copy-start.31
  265.6 2.7 copy-start.32
  267.9 2.6 copy-start.9
  268.3 3.2 copy-start.15
  281.8 4.0 %copy-start.21 = (bf16[256,768]{0,1:T(8,128)(2,1)S(1)}, bf16[256,768]{0,1:T(8,128)(2,1)}, u32[]{:S(2)}) copy-start(bf16[256,768]{0,1:T(8,128)(2,1)} %copy.59) | copy-start | bytes 1179652
  281.8 4.0 %copy-start.38 = (pred[1184]{0:T(1024)(128)(4,1)S(1)}, pred[1184]{0:T(1024)(128)(4,1)}, u32[]{:S(2)}) copy-start(pred[1184]{0:T(1024)(128)(4,1)} %concatenate.41) | copy-start | bytes 3556
  301.9 9.8 %copy-start.28 = (f32[1536]{0:T(1024)S(1)}, f32[1536]{0:T(1024)}, u32[]{:S(2)}) copy-start(f32[1536]{0:T(1024)} %copy-done.27) | copy-start | bytes 18436
  301.9 9.8 %copy-start.30 = (f32[1536]{0:T(1024)S(1)}, f32[1536]{0:T(1024)}, u32[]{:S(2)}) copy-start(f32[1536]{0:T(1024)} %copy-done.29) | copy-start | bytes 18436
  303.8 7.2 %copy-start.10 = (bf16[256,1536]{1,0:T(8,128)(2,1)}, bf16[256,1536]{1,0:T(8,128)(2,1)S(1)}, u32[]{:S(2)}) copy-start(bf16[256,1536]{1,0:T(8,128)(2,1)S(1)} %fusion.22) | copy-start | bytes 2359300
  303.8 7.2 %collective-permute-start.5 = (bf16[256,1536]{1,0:T(8,128)(2,1)S(1)}, bf16[256,1536]{1,0:T(8,128)(2,1)S(1)}, u32[]{:S(2)}, u32[]{:S(2)}) collective-permute-start(bf16[256,1536]{1,0:T(8,128)(2,1)S(1)} %fusion.22), channel_id=1, source_target_pairs={{0,128},{1,129},{2,130},{3,131},{4,132},{5,133},{6,134},{7,135},{8... | collective-permute-start | bytes 2359304 | tf_op jit(solution)/shard_map/ppermute | solution.py:16
  306.5 51.8 %collective-permute-start.4 = (bf16[256,768]{1,0:T(8,128)(2,1)}, bf16[256,768]{1,0:T(8,128)(2,1)}, u32[]{:S(2)}, u32[]{:S(2)}) collective-permute-start(bf16[256,768]{1,0:T(8,128)(2,1)} %slice.293), channel_id=1, source_target_pairs={{128,0},{129,1},{130,2},{131,3},{132,4},{133,5},{134,6},{135,7},{1... | collective-permute-start | bytes 1179656 | tf_op jit(solution)/shard_map/ppermute | solution.py:16
  311.1 5.9 %copy-start.7 = (bf16[256,1536]{1,0:T(8,128)(2,1)}, bf16[256,1536]{1,0:T(8,128)(2,1)S(1)}, u32[]{:S(2)}) copy-start(bf16[256,1536]{1,0:T(8,128)(2,1)S(1)} %collective-permute-done.5) | copy-start | bytes 2359300
  311.6 5.3 %copy-start.17 = (bf16[256,2304]{1,0:T(8,128)(2,1)S(1)}, bf16[256,2304]{1,0:T(8,128)(2,1)}, u32[]{:S(2)}) copy-start(bf16[256,2304]{1,0:T(8,128)(2,1)} %copy-done.16) | copy-start | bytes 3538948
  319.3 3.0 copy-start.1
  331.4 4.1 %copy-start.20 = (bf16[256,768]{0,1:T(8,128)(2,1)S(1)}, bf16[256,768]{0,1:T(8,128)(2,1)}, u32[]{:S(2)}) copy-start(bf16[256,768]{0,1:T(8,128)(2,1)} %copy.62) | copy-start | bytes 1179652
  342.8 8.8 %copy-start.8 = (bf16[256,1536]{1,0:T(8,128)(2,1)S(1)}, bf16[256,1536]{1,0:T(8,128)(2,1)}, u32[]{:S(2)}) copy-start(bf16[256,1536]{1,0:T(8,128)(2,1)} %copy-done.7) | copy-start | bytes 2359300
  342.8 8.8 %copy-start.23 = (f32[1536]{0:T(1024)S(1)}, f32[1536]{0:T(1024)}, u32[]{:S(2)}) copy-start(f32[1536]{0:T(1024)} %get-tuple-element.16) | copy-start | bytes 18436
  351.6 3.9 %copy-start.34 = (f32[2,2]{1,0:T(2,128)S(1)}, f32[2,2]{1,0:T(2,128)}, u32[]{:S(2)}) copy-start(f32[2,2]{1,0:T(2,128)} %param.21) | copy-start | bytes 52
  353.3 5.1 %copy-start.5 = (bf16[2,256,1536]{2,1,0:T(8,128)(2,1)S(1)}, bf16[2,256,1536]{2,1,0:T(8,128)(2,1)}, u32[]{:S(2)}) copy-start(bf16[2,256,1536]{2,1,0:T(8,128)(2,1)} %param.12) | copy-start | bytes 4718596
  353.3 5.1 %copy-start.11 = (bf16[256,1536]{1,0:T(8,128)(2,1)S(1)}, bf16[256,1536]{1,0:T(8,128)(2,1)}, u32[]{:S(2)}) copy-start(bf16[256,1536]{1,0:T(8,128)(2,1)} %copy-done.10) | copy-start | bytes 2359300
  354.1 4.3 %copy-start.13 = (bf16[256,1536]{1,0:T(8,128)(2,1)S(1)}, bf16[256,1536]{1,0:T(8,128)(2,1)}, u32[]{:S(2)}) copy-start(bf16[256,1536]{1,0:T(8,128)(2,1)} %copy-done.12) | copy-start | bytes 2359300
  354.1 4.3 %collective-permute-start.6 = (bf16[256,768]{1,0:T(8,128)(2,1)}, bf16[256,768]{1,0:T(8,128)(2,1)S(1)}, u32[]{:S(2)}, u32[]{:S(2)}) collective-permute-start(bf16[256,768]{1,0:T(8,128)(2,1)} %slice.298), channel_id=1, source_target_pairs={{128,0},{129,1},{130,2},{131,3},{132,4},{133,5},{134,6},{135,7},{1... | collective-permute-start | bytes 1179656 | tf_op jit(solution)/shard_map/ppermute | solution.py:16
  (2 other events, 1.9 us)
Sparse Core Ops, SparseCore 0:
  21.2 107.4 all-gather.1
